TPU v7x, 32 devices: a whole 2x2x4 slice. The times are simulated.
32 devices in a mesh: grp: 4 (over z), mem: 8 (over y, x, core).
Axes of the slice: x: 2, y: 2, z: 4, core: 2. Of those that a mesh axis runs over, the one named last changes fastest.
Arguments:
- design: bfloat16 [8192, 1024], P(('grp', 'mem'))
- active_blocks: int32 [32, 8], P(('grp', 'mem')), may hold values from 0 to 31, as said below
- ridge: float32 [4096], replicated, may hold values from 0.5 to 2
Outputs:
- factored: float32 [8, 128, 128, 128], P('mem', 'grp')
Inputs may be any that keep to these rules, and one draw needn't show every extreme that they name: active_blocks[d, a] % 8 == a for every device d and position a, so a device's blocks are distinct.
All inputs are finite; a program needn't handle non-finite values.
Results may differ from a plain program's by a relative error of at most 0.0003.
Values sent between devices are 32-bit elements; how exact they have to be, the bound alone decides.
No kernel may reach another device: no remote copies, remote signals or barrier semaphores. Data moves between devices by JAX's collectives and lax.ppermute only.
A program may use at most 64 MiB of HBM per device.

v0:
```python
import jax
import jax.numpy as jnp
from jax import lax
from jax.sharding import PartitionSpec as P

NB = 32
BLK = 128
ACT = 8
HI = lax.Precision.HIGHEST


def panel_solve(column):
    count = column.shape[0]
    chol = jnp.linalg.cholesky(column[0])
    stacked = jnp.transpose(column, (2, 0, 1)).reshape(BLK, count * BLK)
    solved = lax.linalg.triangular_solve(chol, stacked, left_side=True, lower=True)
    lower_col = jnp.transpose(solved.reshape(BLK, count, BLK), (1, 2, 0))
    return lower_col.at[0].set(chol)


def apply_step(tiles, lower_col, step, tile_rows, tile_cols):
    left_tiles = jnp.take(lower_col, jnp.maximum(tile_rows - step, 0), axis=0)
    right_tiles = jnp.take(lower_col, jnp.maximum(tile_cols - step, 0), axis=0)
    update = jnp.einsum("tpr,tqr->tpq", left_tiles, right_tiles, precision=HI)
    trailing = ((tile_rows > step) & (tile_cols > step))[:, None, None]
    on_column = ((tile_cols == step) & (tile_rows >= step))[:, None, None]
    on_row = ((tile_rows == step) & (tile_cols > step))[:, None, None]
    tiles = jnp.where(trailing, tiles - update, tiles)
    tiles = jnp.where(on_column, left_tiles, tiles)
    tiles = jnp.where(on_row, jnp.transpose(right_tiles, (0, 2, 1)), tiles)
    return tiles


def column_picker(step, tile_rows, tile_cols):
    wanted = step + jnp.arange(NB - step, dtype=jnp.int32)
    inside = (tile_cols == step) & (tile_rows >= step)
    return ((tile_rows[None, :] == wanted[:, None]) & inside[None, :]).astype(jnp.float32)


def on_device_general(design, active_blocks, ridge):
    n_mem = lax.axis_size("mem")
    n_grp = lax.axis_size("grp")
    member = lax.axis_index("mem")
    group = lax.axis_index("grp")
    classes = n_mem // 8
    per_pos = ACT // classes
    per_row = NB // ACT
    slot_count = NB // classes * per_row
    owned_count = slot_count // n_grp
    row_count = design.shape[0]
    residue = member // 8
    position = member % 8
    everyone = lax.all_gather(active_blocks, "mem", axis=0, tiled=True)
    blocks = design.reshape(row_count, ACT, BLK)
    left = blocks.reshape(row_count, per_pos, classes, BLK)
    outgoing = jnp.einsum("ncqk,nbl->qbckl", left, blocks, preferred_element_type=jnp.float32)
    outgoing = outgoing.reshape(n_mem, per_pos, BLK, BLK)
    received = lax.all_to_all(outgoing, "mem", split_axis=0, concat_axis=0, tiled=True)
    row_ids = jnp.take(everyone.reshape(n_mem, per_pos, classes), residue, axis=2)
    col_ids = jnp.take(everyone, position, axis=1)
    targets = row_ids // classes * per_row + (col_ids // 8)[:, None]
    onehot = (
        targets.reshape(-1)[None, :] == jnp.arange(slot_count, dtype=jnp.int32)[:, None]
    ).astype(jnp.float32)
    sums = jnp.dot(
        onehot,
        received.reshape(n_mem * per_pos, BLK * BLK),
        precision=HI,
        preferred_element_type=jnp.float32,
    )
    sums = sums.reshape(slot_count, BLK, BLK)
    owned = lax.psum_scatter(sums, "grp", scatter_dimension=0, tiled=True)
    slots = group * owned_count + jnp.arange(owned_count, dtype=jnp.int32)
    tile_rows = slots // per_row * classes + residue
    tile_cols = slots % per_row * 8 + position
    ridge_blocks = jnp.take(ridge.reshape(NB, BLK), tile_rows, axis=0)
    same = (tile_rows == tile_cols).astype(jnp.float32)
    extra = jnp.eye(BLK, dtype=jnp.float32)[None] * ridge_blocks[:, None, :] * same[:, None, None]
    divisor = jnp.float32(row_count * n_grp * n_mem // 16)
    tiles = owned / divisor + extra
    picker = column_picker(0, tile_rows, tile_cols)
    partial_value = jnp.einsum("it,tpq->ipq", picker, tiles, precision=HI)
    column = lax.psum(partial_value, ("grp", "mem"))
    lower_col = panel_solve(column)
    tiles = apply_step(tiles, lower_col, 0, tile_rows, tile_cols)
    return tiles[None]


def on_device_fast(design, active_blocks, ridge):
    n_mem = lax.axis_size("mem")
    n_grp = lax.axis_size("grp")
    member = lax.axis_index("mem")
    group = lax.axis_index("grp")
    per_row = NB // ACT
    row_count = design.shape[0]
    divisor = jnp.float32(row_count * n_grp * n_mem // 16)
    eye = jnp.eye(BLK, dtype=jnp.float32)
    ridge_blocks = ridge.reshape(NB, BLK)
    everyone = lax.all_gather(active_blocks, "mem", axis=0, tiled=True)
    blocks = design.reshape(row_count, ACT, BLK)
    outgoing = jnp.einsum("nak,nbl->bakl", blocks, blocks, preferred_element_type=jnp.float32)
    mine00 = jnp.where(active_blocks[0, 0] == 0, outgoing[0, 0], 0.0)
    gram00 = lax.psum(mine00, ("grp", "mem"))
    a00 = gram00 / divisor + eye * ridge_blocks[0][None, :]
    chol = jnp.linalg.cholesky(a00)
    chol_inv = lax.linalg.triangular_solve(chol, eye, left_side=True, lower=True)
    received = lax.all_to_all(outgoing, "mem", split_axis=0, concat_axis=0, tiled=True)
    received = received.reshape(n_mem, ACT, BLK, BLK)
    row_grp = everyone // 8
    col_grp = jnp.take(everyone, member, axis=1) // 8
    grp_ids = jnp.arange(n_grp, dtype=jnp.int32)
    q_ids = jnp.arange(per_row, dtype=jnp.int32)
    mask = (
        (row_grp[:, :, None, None] == grp_ids[None, None, :, None])
        & (col_grp[:, None, None, None] == q_ids[None, None, None, :])
    ).astype(jnp.float32)
    main = jnp.einsum("sagq,sakl->gaqkl", mask, received, precision=HI)
    main = main.reshape(n_grp, ACT * per_row, BLK, BLK)
    col_mask = ((col_grp[:, None] == grp_ids[None, :]) & (everyone[:, 0:1] == 0)).astype(
        jnp.float32
    )
    col_part = jnp.einsum("sg,slk->gkl", col_mask, received[:, 0], precision=HI)
    send = jnp.concatenate([main, col_part[:, None]], axis=1)
    send = send.reshape(n_grp * (ACT * per_row + 1), BLK, BLK)
    got = lax.psum_scatter(send, "grp", scatter_dimension=0, tiled=True)
    owned = got[: ACT * per_row]
    col_tile = got[ACT * per_row] / divisor
    t = jnp.arange(ACT * per_row, dtype=jnp.int32)
    tile_rows = group * 8 + t // per_row
    tile_cols = t % per_row * 8 + member
    same = (tile_rows == tile_cols).astype(jnp.float32)
    diag = eye[None] * jnp.take(ridge_blocks, tile_rows, axis=0)[:, None, :] * same[:, None, None]
    tiles = owned / divisor + diag
    col_rows = lax.all_gather(col_tile, "mem", axis=0, tiled=False)
    col_cols = lax.all_gather(col_tile, "grp", axis=0, tiled=False)
    p_rows = jnp.einsum("ipr,qr->ipq", col_rows, chol_inv, precision=HI)
    p_cols = jnp.einsum("ipr,qr->ipq", col_cols, chol_inv, precision=HI)
    row_ids = group * 8 + jnp.arange(8, dtype=jnp.int32)
    col_ids = jnp.arange(per_row, dtype=jnp.int32) * 8 + member
    p_rows = jnp.where((row_ids == 0)[:, None, None], chol[None], p_rows)
    p_cols = jnp.where((col_ids == 0)[:, None, None], chol[None], p_cols)
    update = jnp.einsum("apr,qsr->aqps", p_rows, p_cols, precision=HI)
    update = update.reshape(ACT * per_row, BLK, BLK)
    left_tiles = jnp.repeat(p_rows, per_row, axis=0)
    right_tiles = jnp.tile(p_cols, (ACT, 1, 1))
    trailing = ((tile_rows > 0) & (tile_cols > 0))[:, None, None]
    on_column = (tile_cols == 0)[:, None, None]
    on_row = ((tile_rows == 0) & (tile_cols > 0))[:, None, None]
    tiles = jnp.where(trailing, tiles - update, tiles)
    tiles = jnp.where(on_column, left_tiles, tiles)
    tiles = jnp.where(on_row, jnp.transpose(right_tiles, (0, 2, 1)), tiles)
    return tiles[None]


def solution(mesh):
    n_mem = mesh.shape["mem"]
    n_grp = mesh.shape["grp"]
    fast = n_mem == 8 and n_grp * 8 == NB
    body = on_device_fast if fast else on_device_general
    in_specs = (P(("grp", "mem"), None), P(("grp", "mem"), None), P())
    out_specs = P("mem", "grp", None, None)
    return jax.shard_map(body, mesh=mesh, in_specs=in_specs, out_specs=out_specs, check_vma=False)
```

profile of v0, /device:TPU:0, one launch (start us, length us, event | category | flops | bytes accessed | tf_op | source)
XLA Modules:
  0.0 329.3 jit_solution(12028579138386191531)
XLA Ops:
  7.4 1.1 copy.56
  8.5 3.8 %convolution_bitcast_fusion.1 = f32[8,8,128,128]{3,2,1,0:T(8,128)} fusion(bf16[256,8,128,1]{2,1,0,3:T(8,128)(2,1)S(1)} %bitcast.82, bf16[256,1024]{1,0:T(8,128)(2,1)} %param.3), kind=kOutput, calls=%fused_computation.5 | convolution fusion | flops 536870912 | bytes 5242880 | tf_op jit(solution)/shard_map/nak,nbl->bakl/dot_general | solution.py:101
  12.3 5.3 %all-to-all-start = ((f32[8,8,128,128]{3,2,1,0:T(8,128)}), f32[8,8,128,128]{3,2,1,0:T(8,128)}, u32[]{:S(2)}, u32[]{:S(2)}) async-start(f32[8,8,128,128]{3,2,1,0:T(8,128)} %convolution_bitcast_fusion.1), calls=%async_computation | async-start | bytes 8388608 | tf_op jit(solution)/shard_map/all_to_all | solution.py:107
  17.7 1.5 fusion.10
  19.2 50.7 %all-gather = s32[8,1,8]{2,1,0:T(1,128)S(1)} all-gather(s32[1,1,8]{2,1,0:T(1,128)S(1)} %bitcast.87), channel_id=1, replica_groups=mesh['grp'=4,'mem'=8] {'mem'}, dimensions={0}, use_global_device_ids=true | all-gather | bytes 288 | tf_op jit(solution)/shard_map/all_gather | solution.py:99
  70.0 0.3 fusion.19
  70.3 0.1 fusion.21
  70.5 1.1 slice_bitcast_fusion
  71.6 0.7 convolution_bitcast_fusion.3
  72.2 0.1 copy.43
  72.4 14.0 %convolution_bitcast_fusion = f32[4,8,4,128,128]{4,2,0,3,1:T(4,128)S(1)} fusion(f32[8,8,128,128,1]{3,2,1,0,4:T(8,128)} %bitcast.6, pred[8,4]{0,1:T(4,128)(4,1)S(1)} %iota_compare_fusion.4, pred[8,8,4]{0,2,1:T(4,128)(4,1)S(1)} %iota_compare_fusion.3), kind=kOutput, calls=%fused_computation.2 | convolution fusion | flops 201327616 | bytes 12583200 | tf_op jit(solution)/shard_map/sagq,sakl->gaqkl/dot_general | solution.py:117
  86.4 2.7 copy.41
  89.1 3.9 %pad_maximum_fusion = f32[4,33,128,128]{3,2,1,0:T(8,128)} fusion(f32[4,1,128,128]{3,2,1,0:T(8,128)S(1)} %copy.43, f32[4,32,128,128]{3,2,1,0:T(8,128)S(1)} %bitcast.80), kind=kLoop, calls=%fused_computation.1 | loop fusion | flops 2162688 | bytes 17301504 | tf_op jit(solution)/shard_map/concatenate | solution.py:123
  93.1 0.7 copy-done
  93.8 0.6 gather_fusion
  94.5 167.3 %all-reduce.2.cloned.1.call-done = f32[128,128]{1,0:T(8,128)} async-done(((f32[128,128]{1,0:T(8,128)}), f32[128,128]{1,0:T(8,128)}) %all-reduce.2.cloned.1.call-update) | async-done | bytes 65552 | tf_op jit(solution)/shard_map/psum | solution.py:103
  261.8 0.9 select_add_fusion
  262.8 0.9 fusion.12
  263.7 11.7 %cholesky.23 = f32[128,128]{1,0:T(8,128)S(1)} custom-call(f32[128,128]{1,0:T(8,128)S(1)} %fusion.12), custom_call_target="Cholesky" | custom-call | tf_op jit(solution)/shard_map/jit(cholesky)/cholesky | solution.py:105
  275.4 0.6 compare_reduce_fusion
  276.1 0.7 select_bitcast_fusion
  276.7 9.8 %custom-call.6 = f32[1,128,128]{1,2,0:T(8,128)S(1)} custom-call(f32[1,128,128]{2,1,0:T(8,128)S(1)} %get-tuple-element.16), custom_call_target="InvertDiagBlocksLowerTriangular" | custom-call | tf_op jit(solution)/shard_map/triangular_solve | solution.py:106
  286.5 0.2 convolution_bitcast_fusion.4
  286.8 0.8 slice_multiply_fusion.1
  287.7 15.1 %all_gather.12 = f32[4,128,128]{2,1,0:T(8,128)S(1)} all-gather(f32[1,128,128]{2,1,0:T(8,128)S(1)} %slice_multiply_fusion.1), channel_id=1, replica_groups=mesh['grp'=4,'mem'=8] {'grp'}, dimensions={0}, use_global_device_ids=true | all-gather | bytes 327680 | tf_op jit(solution)/shard_map/all_gather | solution.py:135
  302.8 10.0 %all_gather.13 = f32[8,128,128]{2,1,0:T(8,128)S(1)} all-gather(f32[1,128,128]{2,1,0:T(8,128)S(1)} %slice_multiply_fusion.1), channel_id=1, replica_groups=mesh['grp'=4,'mem'=8] {'mem'}, dimensions={0}, use_global_device_ids=true | all-gather | bytes 589824 | tf_op jit(solution)/shard_map/all_gather | solution.py:134
  312.8 0.4 convolution_select_fusion.1
  313.2 0.1 copy.44
  313.3 0.6 convolution_select_fusion
  313.9 1.8 convolution_bitcast_fusion.2
  315.7 1.9 copy.45
  317.6 4.3 %fusion.3 = f32[1,32,128,128]{3,2,1,0:T(8,128)} fusion(f32[33,128,128]{2,1,0:T(8,128)} %reduce-scatter.2.cloned.1.call-done, f32[8,4,128,128]{3,2,1,0:T(8,128)} %copy.45, f32[32]{0:T(128)S(1)} %get-tuple-element.18, f32[32,128]{1,0:T(8,128)S(1)} %broadcast_select_fusion, f32[128,128]{1,0:T(8,128)S(1)} %fusion.13, ...), kind=kLoop, calls=%fused_computation.8 | loop fusion | flops 4194304 | bytes 7160032 | tf_op jit(solution)/shard_map/broadcast_in_dim | solution.py:152
  (26 shorter events, 0.5 us)
Async XLA Ops:
  12.3 5.3 %copy-start.1 = (s32[1,8]{1,0:T(1,128)S(1)}, s32[1,8]{1,0:T(1,128)}, u32[]{:S(2)}) copy-start(s32[1,8]{1,0:T(1,128)} %param.4) | copy-start | bytes 100
  12.3 58.2 %all-to-all-start = ((f32[8,8,128,128]{3,2,1,0:T(8,128)}), f32[8,8,128,128]{3,2,1,0:T(8,128)}, u32[]{:S(2)}, u32[]{:S(2)}) async-start(f32[8,8,128,128]{3,2,1,0:T(8,128)} %convolution_bitcast_fusion.1), calls=%async_computation | async-start | bytes 8388608 | tf_op jit(solution)/shard_map/all_to_all | solution.py:107
  17.6 244.3 %all-reduce.2.cloned.1.call-start = ((), (), s32[]{:S(2)}) async-start(), calls=%async_computation.2 | async-start | bytes 131072 | tf_op jit(solution)/shard_map/psum | solution.py:103
  19.2 267.6 %reduce-scatter.2.cloned.1.call-start = ((), (), s32[]{:S(2)}) async-start(), calls=%async_computation.3 | async-start | bytes 10813440 | tf_op jit(solution)/shard_map/reduce_scatter | solution.py:125
  93.0 0.7 copy-start
Sparse Core Ops, SparseCore 0:
  24.0 237.8 all-reduce.1
Sparse Core Ops, SparseCore 1:
  93.1 149.5 reduce-scatter.1
where the time goes:
time: 330 us; the launch traced here: 329 us
  waiting for transfers between devices  167 us (51%)
  blocking collectives  75.8 us (23%)
  other arithmetic  35.7 us (11%)
  matrix products  21.5 us (7%)
  between operations  15.1 us (5%)
  local copies, waits for them, and re-layouts  8.48 us (3%)
  starting transfers between devices  5.37 us (2%)
    psum x1, waiting for transfers between devices, on_device_fast(): gram00 = lax.psum(mine00, ('grp', 'mem'))  167 us
    all_gather x1, blocking collectives, on_device_fast(): everyone = lax.all_gather(active_blocks, 'mem', axis=0, tiled=True)  50.7 us
    all_gather x1, blocking collectives, on_device_fast(): col_cols = lax.all_gather(col_tile, 'grp', axis=0, tiled=False)  15.1 us
    dot_general x1, matrix products, on_device_fast(): main = jnp.einsum('sagq,sakl->gaqkl', mask, received, precision=HI)  14 us
    another operation x3, other arithmetic, on_device_fast(): chol = jnp.linalg.cholesky(a00)  12.4 us
    another operation x2, other arithmetic, on_device_fast(): lax.linalg.triangular_solve(chol, eye, left_side=True, lower=True)  10.5 us
    all_gather x1, blocking collectives, on_device_fast(): col_rows = lax.all_gather(col_tile, 'mem', axis=0, tiled=False)  10 us
  transfers between devices with their start and end apart: 3, of which 1 were waited for; matrix products, arithmetic and copies ran while one was open for 15% of the time, Pallas kernels for 0%

commit v1 on v0

--- a/solution.py
+++ b/solution.py
@@ -7,6 +7,11 @@
 BLK = 128
 ACT = 8
 HI = lax.Precision.HIGHEST
+
+
+def by_each_axis(value, axis_one, axis_two):
+    half = lax.psum(value, axis_one)
+    return lax.psum(half, axis_two)
 
 
 def panel_solve(column):
@@ -100,7 +105,7 @@
     blocks = design.reshape(row_count, ACT, BLK)
     outgoing = jnp.einsum("nak,nbl->bakl", blocks, blocks, preferred_element_type=jnp.float32)
     mine00 = jnp.where(active_blocks[0, 0] == 0, outgoing[0, 0], 0.0)
-    gram00 = lax.psum(mine00, ("grp", "mem"))
+    gram00 = by_each_axis(mine00, "mem", "grp")
     a00 = gram00 / divisor + eye * ridge_blocks[0][None, :]
     chol = jnp.linalg.cholesky(a00)
     chol_inv = lax.linalg.triangular_solve(chol, eye, left_side=True, lower=True)

time: 330 us -> 314 us (0.952)
  waiting for transfers between devices: 167 us -> 153 us
    psum x1 -> x2, waiting for transfers between devices: 167 us -> 27.6 us  [the longest x1 15.8 us: by_each_axis(): half = lax.psum(value, axis_one)]
    reduce_scatter x1, waiting for transfers between devices: 0.03 us -> 126 us  [on_device_fast(): got = lax.psum_scatter(send, 'grp', scatter_dimension=0, tiled=True)]
  transfers between devices with their start and end apart: 3 -> 4, of which waited for: 1 -> 3; matrix products, arithmetic and copies ran while one was open for 15% -> 16% of each run, Pallas kernels for 0% -> 0%
where the time goes in v1:
time: 314 us
  waiting for transfers between devices  153 us (49%)
  blocking collectives  75.8 us (24%)
  other arithmetic  35.7 us (11%)
  matrix products  21.4 us (7%)
  between operations  13.3 us (4%)
  local copies, waits for them, and re-layouts  8.48 us (3%)
  starting transfers between devices  5.41 us (2%)
    reduce_scatter x1, waiting for transfers between devices, on_device_fast(): got = lax.psum_scatter(send, 'grp', scatter_dimension=0, tiled=True)  126 us
    all_gather x1, blocking collectives, on_device_fast(): everyone = lax.all_gather(active_blocks, 'mem', axis=0, tiled=True)  51 us
    psum x1, waiting for transfers between devices, by_each_axis(): half = lax.psum(value, axis_one)  15.8 us
    all_gather x1, blocking collectives, on_device_fast(): col_cols = lax.all_gather(col_tile, 'grp', axis=0, tiled=False)  14.7 us
    dot_general x1, matrix products, on_device_fast(): main = jnp.einsum('sagq,sakl->gaqkl', mask, received, precision=HI)  14 us
    another operation x3, other arithmetic, on_device_fast(): chol = jnp.linalg.cholesky(a00)  12.4 us
    psum x1, waiting for transfers between devices, by_each_axis(): return lax.psum(half, axis_two)  11.7 us
    another operation x2, other arithmetic, on_device_fast(): lax.linalg.triangular_solve(chol, eye, left_side=True, lower=True)  10.5 us
  transfers between devices with their start and end apart: 4, of which 3 were waited for; matrix products, arithmetic and copies ran while one was open for 16% of the time, Pallas kernels for 0%

profile of v1, /device:TPU:0, one launch (start us, length us, event | category | flops | bytes accessed | tf_op | source)
XLA Modules:
  0.0 313.6 jit_solution(16948941735167242482)
XLA Ops:
  6.5 1.1 copy.56
  7.7 3.8 %convolution_bitcast_fusion.1 = f32[8,8,128,128]{3,2,1,0:T(8,128)} fusion(bf16[256,8,128,1]{2,1,0,3:T(8,128)(2,1)S(1)} %bitcast.82, bf16[256,1024]{1,0:T(8,128)(2,1)} %param.3), kind=kOutput, calls=%fused_computation.5 | convolution fusion | flops 536870912 | bytes 5242880 | tf_op jit(solution)/shard_map/nak,nbl->bakl/dot_general | solution.py:106
  11.4 5.3 %all-to-all-start = ((f32[8,8,128,128]{3,2,1,0:T(8,128)}), f32[8,8,128,128]{3,2,1,0:T(8,128)}, u32[]{:S(2)}, u32[]{:S(2)}) async-start(f32[8,8,128,128]{3,2,1,0:T(8,128)} %convolution_bitcast_fusion.1), calls=%async_computation | async-start | bytes 8388608 | tf_op jit(solution)/shard_map/all_to_all | solution.py:112
  16.8 1.5 fusion.10
  18.4 51.0 %all-gather = s32[8,1,8]{2,1,0:T(1,128)S(1)} all-gather(s32[1,1,8]{2,1,0:T(1,128)S(1)} %bitcast.87), channel_id=1, replica_groups=mesh['grp'=4,'mem'=8] {'mem'}, dimensions={0}, use_global_device_ids=true | all-gather | bytes 288 | tf_op jit(solution)/shard_map/all_gather | solution.py:104
  69.5 0.3 fusion.19
  69.9 15.8 %all-reduce.3.cloned.1.call-done = f32[128,128]{1,0:T(8,128)} async-done(((f32[128,128]{1,0:T(8,128)}), f32[128,128]{1,0:T(8,128)}) %all-reduce.3.cloned.1.call-update) | async-done | bytes 65552 | tf_op jit(solution)/shard_map/psum | solution.py:13
  85.9 1.1 slice_bitcast_fusion
  86.9 0.7 convolution_bitcast_fusion.3
  87.6 0.1 copy.43
  87.7 14.0 %convolution_bitcast_fusion = f32[4,8,4,128,128]{4,2,0,3,1:T(4,128)S(1)} fusion(f32[8,8,128,128,1]{3,2,1,0,4:T(8,128)} %bitcast.6, pred[8,4]{0,1:T(4,128)(4,1)S(1)} %iota_compare_fusion.4, pred[8,8,4]{0,2,1:T(4,128)(4,1)S(1)} %iota_compare_fusion.3), kind=kOutput, calls=%fused_computation.2 | convolution fusion | flops 201327616 | bytes 12583200 | tf_op jit(solution)/shard_map/sagq,sakl->gaqkl/dot_general | solution.py:122
  101.8 2.7 copy.41
  104.5 3.9 %pad_maximum_fusion = f32[4,33,128,128]{3,2,1,0:T(8,128)} fusion(f32[4,1,128,128]{3,2,1,0:T(8,128)S(1)} %copy.43, f32[4,32,128,128]{3,2,1,0:T(8,128)S(1)} %bitcast.80), kind=kLoop, calls=%fused_computation.1 | loop fusion | flops 2162688 | bytes 17301504 | tf_op jit(solution)/shard_map/concatenate | solution.py:128
  108.4 0.7 copy-done
  109.1 0.6 gather_fusion
  109.9 11.7 %all-reduce.5.cloned.1.call-done = f32[128,128]{1,0:T(8,128)} async-done(((f32[128,128]{1,0:T(8,128)}), f32[128,128]{1,0:T(8,128)}) %all-reduce.5.cloned.1.call-update) | async-done | bytes 65552 | tf_op jit(solution)/shard_map/psum | solution.py:14
  121.6 0.9 select_add_fusion
  122.6 0.9 fusion.12
  123.4 11.7 %cholesky.23 = f32[128,128]{1,0:T(8,128)S(1)} custom-call(f32[128,128]{1,0:T(8,128)S(1)} %fusion.12), custom_call_target="Cholesky" | custom-call | tf_op jit(solution)/shard_map/jit(cholesky)/cholesky | solution.py:110
  135.2 0.6 compare_reduce_fusion
  135.8 0.7 select_bitcast_fusion
  136.5 9.8 %custom-call.6 = f32[1,128,128]{1,2,0:T(8,128)S(1)} custom-call(f32[1,128,128]{2,1,0:T(8,128)S(1)} %get-tuple-element.16), custom_call_target="InvertDiagBlocksLowerTriangular" | custom-call | tf_op jit(solution)/shard_map/triangular_solve | solution.py:111
  146.3 0.2 convolution_bitcast_fusion.4
  146.5 125.8 %reduce-scatter.2.cloned.1.call-done = f32[33,128,128]{2,1,0:T(8,128)} async-done(((f32[132,128,128]{2,1,0:T(8,128)}), f32[33,128,128]{2,1,0:T(8,128)}) %reduce-scatter.2.cloned.1.call-update) | async-done | bytes 2162704 | tf_op jit(solution)/shard_map/reduce_scatter | solution.py:130
  272.3 0.8 slice_multiply_fusion.1
  273.2 14.7 %all_gather.12 = f32[4,128,128]{2,1,0:T(8,128)S(1)} all-gather(f32[1,128,128]{2,1,0:T(8,128)S(1)} %slice_multiply_fusion.1), channel_id=1, replica_groups=mesh['grp'=4,'mem'=8] {'grp'}, dimensions={0}, use_global_device_ids=true | all-gather | bytes 327680 | tf_op jit(solution)/shard_map/all_gather | solution.py:140
  287.9 10.1 %all_gather.13 = f32[8,128,128]{2,1,0:T(8,128)S(1)} all-gather(f32[1,128,128]{2,1,0:T(8,128)S(1)} %slice_multiply_fusion.1), channel_id=1, replica_groups=mesh['grp'=4,'mem'=8] {'mem'}, dimensions={0}, use_global_device_ids=true | all-gather | bytes 589824 | tf_op jit(solution)/shard_map/all_gather | solution.py:139
  298.0 0.4 convolution_select_fusion.1
  298.5 0.6 convolution_select_fusion
  299.1 1.8 convolution_bitcast_fusion.2
  300.9 1.9 copy.45
  302.8 4.3 %fusion.3 = f32[1,32,128,128]{3,2,1,0:T(8,128)} fusion(f32[33,128,128]{2,1,0:T(8,128)} %reduce-scatter.2.cloned.1.call-done, f32[8,4,128,128]{3,2,1,0:T(8,128)} %copy.45, f32[32]{0:T(128)S(1)} %get-tuple-element.18, f32[32,128]{1,0:T(8,128)S(1)} %broadcast_select_fusion, f32[128,128]{1,0:T(8,128)S(1)} %fusion.13, ...), kind=kLoop, calls=%fused_computation.8 | loop fusion | flops 4194304 | bytes 7160032 | tf_op jit(solution)/shard_map/broadcast_in_dim | solution.py:157
  (29 shorter events, 0.8 us)
Async XLA Ops:
  11.4 5.3 %copy-start.1 = (s32[1,8]{1,0:T(1,128)S(1)}, s32[1,8]{1,0:T(1,128)}, u32[]{:S(2)}) copy-start(s32[1,8]{1,0:T(1,128)} %param.4) | copy-start | bytes 100
  11.4 74.4 %all-to-all-start = ((f32[8,8,128,128]{3,2,1,0:T(8,128)}), f32[8,8,128,128]{3,2,1,0:T(8,128)}, u32[]{:S(2)}, u32[]{:S(2)}) async-start(f32[8,8,128,128]{3,2,1,0:T(8,128)} %convolution_bitcast_fusion.1), calls=%async_computation | async-start | bytes 8388608 | tf_op jit(solution)/shard_map/all_to_all | solution.py:112
  16.7 69.0 %all-reduce.3.cloned.1.call-start = ((), (), s32[]{:S(2)}) async-start(), calls=%async_computation.2 | async-start | bytes 131072 | tf_op jit(solution)/shard_map/psum | solution.py:13
  18.3 103.3 %all-reduce.5.cloned.1.call-start = ((), (), s32[]{:S(2)}) async-start(), calls=%async_computation.3 | async-start | bytes 131072 | tf_op jit(solution)/shard_map/psum | solution.py:14
  85.8 186.5 %reduce-scatter.2.cloned.1.call-start = ((), (), s32[]{:S(2)}) async-start(), calls=%async_computation.4 | async-start | bytes 10813440 | tf_op jit(solution)/shard_map/reduce_scatter | solution.py:130
  108.4 0.7 copy-start
Sparse Core Ops, SparseCore 0:
  20.6 65.1 all-reduce.2
  88.2 33.3 all-reduce.4
  124.0 148.3 reduce-scatter.1
